TPU v7x, 32 devices: a whole 2x2x4 slice. The times are simulated.
32 devices in a mesh: grp: 2 (over y), chan: 4 (over z), tile: 2 (over x), sub: 2 (over core).
Axes of the slice: x: 2, y: 2, z: 4, core: 2. Of those that a mesh axis runs over, the one named last changes fastest.
Arguments:
- dirty: bfloat16 [128, 32, 8, 128], P(('grp', 'chan'), None, ('tile', 'sub')), parts along dimension 0, may hold values from -6 to 6
- cotangent: bfloat16 [128, 32, 8, 128], P(('grp', 'chan'), None, ('tile', 'sub')), parts along dimension 0, may hold values from -6 to 6
- spatial_kernel: float32 [32, 25], replicated, may hold values from -1.25 to 1.25
- feature_mix: bfloat16 [32, 32], replicated, may hold values from -1 to 1
- spectral_kernel: bfloat16 [7, 32, 32], replicated, may hold values from -0.375 to 0.375
- freq_table: int32 [64], replicated, may hold values from 0 to 63, as said below
Outputs:
- restored: bfloat16 [128, 32, 8, 128], P(('grp', 'chan'), None, ('tile', 'sub')), parts along dimension 0
- dirty_grad: bfloat16 [128, 32, 8, 128], P(('grp', 'chan'), None, ('tile', 'sub')), parts along dimension 0
- spatial_grad: float32 [64, 25], P('grp'), parts along dimension 0
- mix_grad: float32 [64, 32], P('grp'), parts along dimension 0
- spectral_grad: float32 [14, 32, 32], P('grp'), parts along dimension 0
There are 2 independent parts, one for each index of `grp`. A program takes and returns all parts, laid end to end along the dimension named above; an argument that names none is the same for every part. Nothing has to cross between parts.
Inputs may be any that keep to these rules, and one draw needn't show every extreme that they name: freq_table is a permutation of 0..63; the stored channels d * 16 to (d+1) * 16 - 1 hold exactly the frequencies m * 4 + d for m in 0..15, in any order.
All inputs are finite; a program needn't handle non-finite values.
Results may differ from a plain program's by a relative error of at most 0.0062.
Values may be sent and summed in bfloat16 or wider, within the bound.
No kernel may reach another device: no remote copies, remote signals or barrier semaphores. Data moves between devices by JAX's collectives and lax.ppermute only.
A program may use at most 64 MiB of HBM per device.

v0:
```python
import math
import jax
import jax.numpy as jnp
from jax import lax
from jax.sharding import PartitionSpec as P


def padded(block, sides, width):
    for axis, dim in sides:
        count = lax.axis_size(axis)
        forward = [(i, i + 1) for i in range(count - 1)]
        backward = [(target, source) for source, target in forward]
        low = lax.ppermute(
            lax.slice_in_dim(block, block.shape[dim] - width, None, axis=dim), axis, forward
        )
        high = lax.ppermute(lax.slice_in_dim(block, 0, width, axis=dim), axis, backward)
        block = jnp.concatenate([low, block, high], axis=dim)
    return block


def passed_along(block, axis, distance):
    devices = range(lax.axis_size(axis))
    route = [((i - distance) % len(devices), i) for i in devices]
    return lax.ppermute(block, axis, route)


def silu_slope(value):
    sig = jax.nn.sigmoid(value)
    return sig * (1.0 + value * (1.0 - sig))


def move_down(array):
    return jnp.pad(array, ((1, 0), (0, 0), (0, 0)))[:-1]


def move_up(array):
    return jnp.pad(array, ((0, 1), (0, 0), (0, 0)))[1:]


def local(dirty, cotangent, spatial_kernel, feature_mix, spectral_kernel, freq_table):
    chans, feats, rows, cols = dirty.shape
    taps = spectral_kernel.shape[0]
    half = (taps - 1) // 2
    n_chan = lax.axis_size("chan")
    n_rows = lax.axis_size("tile") * lax.axis_size("sub")
    scale = 1.0 / math.sqrt(chans * n_chan * rows * n_rows * cols)
    pixels = rows * cols
    extended = padded(dirty, ((("tile", "sub"), 2),), 2)
    xpad = jnp.pad(extended, ((0, 0), (0, 0), (0, 0), (2, 2)))
    xpad32 = xpad.astype(jnp.float32)
    total = jnp.zeros(dirty.shape, jnp.float32)
    for i in range(5):
        for j in range(5):
            total = (
                total
                + spatial_kernel[:, i * 5 + j][None, :, None, None]
                * xpad32[:, :, i : i + rows, j : j + cols]
            )
    smooth = total.astype(jnp.bfloat16)
    mixed = jnp.einsum("gf,cfhw->cghw", feature_mix, smooth, preferred_element_type=jnp.float32)
    hidden = jax.nn.silu(mixed).astype(jnp.bfloat16)
    hidden_flat = hidden.reshape(chans, feats, pixels)
    grad_flat = cotangent.reshape(chans, feats, pixels)
    device = lax.axis_index("chan")
    start = device * chans
    own = lax.dynamic_slice_in_dim(freq_table, start, chans) // n_chan
    order = jnp.zeros((chans,), jnp.int32).at[own].set(jnp.arange(chans, dtype=jnp.int32))
    h_sorted = hidden_flat[order]
    g_sorted = grad_flat[order]
    fwd_acc = jnp.einsum(
        "gf,mfp->mgp", spectral_kernel[half], h_sorted, preferred_element_type=jnp.float32
    )
    bwd_acc = jnp.einsum(
        "gf,mgp->mfp", spectral_kernel[half], g_sorted, preferred_element_type=jnp.float32
    )
    grad_taps = [None] * taps
    grad_taps[half] = jnp.einsum(
        "mgp,mfp->gf", g_sorted, h_sorted, preferred_element_type=jnp.float32
    )
    for dist in range(1, half + 1):
        for sign in (-1, 1):
            h_far, g_far = passed_along((h_sorted, g_sorted), "chan", -sign * dist)
            if sign < 0:
                wrapped = device < dist
                h_near = jnp.where(wrapped, move_down(h_far), h_far)
                g_near = jnp.where(wrapped, move_down(g_far), g_far)
            else:
                wrapped = device + dist >= n_chan
                h_near = jnp.where(wrapped, move_up(h_far), h_far)
                g_near = jnp.where(wrapped, move_up(g_far), g_far)
            offset = sign * dist
            fwd_acc = fwd_acc + jnp.einsum(
                "gf,mfp->mgp",
                spectral_kernel[half + offset],
                h_near,
                preferred_element_type=jnp.float32,
            )
            bwd_acc = bwd_acc + jnp.einsum(
                "gf,mgp->mfp",
                spectral_kernel[half - offset],
                g_near,
                preferred_element_type=jnp.float32,
            )
            grad_taps[half + offset] = jnp.einsum(
                "mgp,mfp->gf", g_sorted, h_near, preferred_element_type=jnp.float32
            )
    spec_grad = jnp.stack(grad_taps, 0)
    spec_flat = fwd_acc.astype(jnp.bfloat16)[own]
    back_flat = bwd_acc.astype(jnp.bfloat16)[own]
    spec = spec_flat.reshape(chans, feats, rows, cols)
    back = back_flat.reshape(chans, feats, rows, cols)
    restored = (dirty.astype(jnp.float32) + spec.astype(jnp.float32)).astype(jnp.bfloat16)
    dmixed = (back.astype(jnp.float32) * silu_slope(mixed)).astype(jnp.bfloat16)
    mix_term = jnp.einsum("cghw,cfhw->gf", dmixed, smooth, preferred_element_type=jnp.float32)
    dsmooth = jnp.einsum(
        "gf,cghw->cfhw", feature_mix, dmixed, preferred_element_type=jnp.float32
    ).astype(jnp.bfloat16)
    grad_ext = padded(dsmooth, ((("tile", "sub"), 2),), 2)
    dpad32 = jnp.pad(grad_ext, ((0, 0), (0, 0), (0, 0), (2, 2))).astype(jnp.float32)
    conv = jnp.zeros(dirty.shape, jnp.float32)
    terms = []
    for i in range(5):
        for j in range(5):
            conv = (
                conv
                + spatial_kernel[:, i * 5 + j][None, :, None, None]
                * dpad32[:, :, 4 - i : 4 - i + rows, 4 - j : 4 - j + cols]
            )
            terms.append(
                jnp.einsum(
                    "cfhw,cfhw->f",
                    dsmooth,
                    xpad[:, :, i : i + rows, j : j + cols],
                    preferred_element_type=jnp.float32,
                )
            )
    kernel_term = jnp.stack(terms, 1)
    dirty_grad = (cotangent.astype(jnp.float32) + conv).astype(jnp.bfloat16)
    kgrad, mgrad, sgrad = lax.psum((kernel_term, mix_term, spec_grad), ("chan", "tile", "sub"))
    return (restored, dirty_grad, kgrad * scale, mgrad * scale, sgrad * scale)


def solution(mesh):
    in_specs = (
        P(("grp", "chan"), None, ("tile", "sub"), None),
        P(("grp", "chan"), None, ("tile", "sub"), None),
        P(),
        P(),
        P(),
        P(),
    )
    out_specs = (
        P(("grp", "chan"), None, ("tile", "sub"), None),
        P(("grp", "chan"), None, ("tile", "sub"), None),
        P("grp", None),
        P("grp", None),
        P("grp", None, None),
    )
    return jax.shard_map(local, mesh=mesh, in_specs=in_specs, out_specs=out_specs, check_vma=False)
```

profile of v0, /device:TPU:0, one launch (start us, length us, event | category | flops | bytes accessed | tf_op | source)
XLA Modules:
  0.0 144.2 jit_solution(15052567029493651229)
XLA Ops:
  0.7 0.8 compare_select_fusion.1
  1.4 0.6 scatter_custom_fusion
  2.1 1.1 reshape.48
  3.8 4.1 %collective-permute-start.7 = (bf16[16,32,256]{2,1,0:T(8,128)(2,1)S(1)}, bf16[16,32,256]{2,1,0:T(8,128)(2,1)S(1)}, u32[]{:S(2)}, u32[]{:S(2)}) collective-permute-start(bf16[16,32,256]{2,1,0:T(8,128)(2,1)S(1)} %gather_fusion.2), channel_id=1, source_target_pairs={{8,0},{12,4},{0,8},{4,12},{9,1},{13,5},{1,9},{5,13},{10,2},{14,6},... | collective-permute-start | bytes 786440 | tf_op jit(solution)/shard_map/ppermute | solution.py:24
  7.9 1.3 collective-permute-start.6
  9.2 0.7 collective-permute-start.5
  9.9 1.0 copy.27
  10.9 1.3 collective-permute-start.1
  12.2 3.0 %collective-permute-start = (bf16[16,32,2,128]{3,1,2,0:T(8,128)(2,1)S(1)}, bf16[16,32,2,128]{3,1,2,0:T(8,128)(2,1)S(1)}, u32[]{:S(2)}, u32[]{:S(2)}) collective-permute-start(bf16[16,32,2,128]{3,1,2,0:T(8,128)(2,1)S(1)} %copy.27), channel_id=1, source_target_pairs={{0,1},{1,2},{2,3},{4,5},{5,6},{6,7},{8,9},{9,10},{10,11},{12,13},{... | collective-permute-start | bytes 786440 | tf_op jit(solution)/shard_map/ppermute | solution.py:13
  15.3 1.2 slice_reduce_fusion.23
  16.5 2.5 %slice_reduce_fusion.24 = (f32[32]{0:T(128)S(1)}, f32[32]{0:T(128)S(1)}, f32[32]{0:T(128)S(1)}, f32[32]{0:T(128)S(1)}, f32[32]{0:T(128)S(1)}, /*index=5*/f32[32]...) fusion(f32[32,25]{1,0:T(8,128)} %param.8), kind=kLoop, calls=%fused_computation.293 | loop fusion | bytes 4864 | tf_op jit(solution)/shard_map/slice | solution.py:56
  19.0 1.0 fusion.159
  20.0 1.5 %collective-permute-done.7 = bf16[16,32,256]{2,1,0:T(8,128)(2,1)S(1)} collective-permute-done((bf16[16,32,256]{2,1,0:T(8,128)(2,1)S(1)}, bf16[16,32,256]{2,1,0:T(8,128)(2,1)S(1)}, u32[]{:S(2)}, u32[]{:S(2)}) %collective-permute-start.7) | collective-permute-done | bytes 262176 | tf_op jit(solution)/shard_map/ppermute | solution.py:24
  21.5 1.0 fusion.109
  22.8 3.9 %collective-permute-done.5 = bf16[16,32,256]{2,1,0:T(8,128)(2,1)S(1)} collective-permute-done((bf16[16,32,256]{2,1,0:T(8,128)(2,1)S(1)}, bf16[16,32,256]{2,1,0:T(8,128)(2,1)S(1)}, u32[]{:S(2)}, u32[]{:S(2)}) %collective-permute-start.5) | collective-permute-done | bytes 262176 | tf_op jit(solution)/shard_map/ppermute | solution.py:24
  28.5 0.8 select_maximum_fusion.2
  29.4 3.0 %fusion.74 = bf16[16,32,2,128]{3,1,2,0:T(8,128)(2,1)S(1)} fusion(f32[16,32,6,132]{3,1,2,0:T(8,128)S(1)} %get-tuple-element.72, f32[32]{0:T(128)S(1)} %get-tuple-element.66, f32[32]{0:T(128)S(1)} %get-tuple-element.67, f32[32]{0:T(128)S(1)} %get-tuple-element.44, f32[32]{0:T(128)S(1)} %get-tuple-element.45, f32[32]{0:T(128)S(1)} %get-tuple-element.46, ...), kind=kLoop, calls=%fused_computation.150 | loop fusion | flops 6553600 | bytes 13372544 | tf_op jit(solution)/shard_map/convert_element_type | solution.py:59
  32.4 1.1 fusion.46
  33.6 0.6 gather_fusion
  34.2 7.2 %collective-permute-start.4 = (bf16[16,32,256]{2,1,0:T(8,128)(2,1)S(1)}, bf16[16,32,256]{2,1,0:T(8,128)(2,1)}, u32[]{:S(2)}, u32[]{:S(2)}) collective-permute-start(bf16[16,32,256]{2,1,0:T(8,128)(2,1)S(1)} %gather_fusion), channel_id=1, source_target_pairs={{8,0},{12,4},{0,8},{4,12},{9,1},{13,5},{1,9},{5,13},{10,2},{14,6},... | collective-permute-start | bytes 786440 | tf_op jit(solution)/shard_map/ppermute | solution.py:24
  41.8 1.6 %collective-permute-start.2 = (bf16[16,32,256]{2,1,0:T(8,128)(2,1)S(1)}, bf16[16,32,256]{2,1,0:T(8,128)(2,1)}, u32[]{:S(2)}, u32[]{:S(2)}) collective-permute-start(bf16[16,32,256]{2,1,0:T(8,128)(2,1)S(1)} %gather_fusion), channel_id=1, source_target_pairs={{12,0},{0,4},{4,8},{8,12},{13,1},{1,5},{5,9},{9,13},{14,2},{2,6},{... | collective-permute-start | bytes 786440 | tf_op jit(solution)/shard_map/ppermute | solution.py:24
  43.6 2.5 %fusion.44 = (f32[32]{0:T(128)}, f32[32]{0:T(128)}, f32[32]{0:T(128)}, f32[32]{0:T(128)}, f32[32]{0:T(128)}, /*index=5*/f32[32]{0:T(128)}, bf16[16,2,128,32]{2,3,1,0:T(8,128)(2,1)S(1)}) fusion(bf16[16,32,6,132]{3,1,2,0:T(8,128)(2,1)S(1)} %get-tuple-element.71, bf16[16,32,2,128]{3,1,2,0:T(8,128)(2,1)} %copy-done.7, ...), kind=kOutput, calls=%fused_computation.93 | convolution fusion | flops 11272000 | bytes 1837824 | tf_op jit(solution)/shard_map/gf,cghw->cfhw/dot_general | solution.py:115
  46.0 2.3 %fusion.45 = (f32[32]{0:T(128)}, f32[32]{0:T(128)}, f32[32]{0:T(128)}, f32[32]{0:T(128)}, f32[32]{0:T(128)}, /*index=5*/f32[32]{0:T(128)}, f32[32]{0:T(128)}, f3...) fusion(bf16[16,32,6,132]{3,1,2,0:T(8,128)(2,1)S(1)} %get-tuple-, ...), kind=kLoop, calls=%fused_computation.94 | loop fusion | flops 7208384 | bytes 4983040 | tf_op jit(solution)/shard_map/cfhw,cfhw->f/dot_general | solution.py:130
  48.4 1.3 collective-permute-start.9
  49.7 3.0 %collective-permute-start.8 = (bf16[16,32,2,128]{3,1,2,0:T(8,128)(2,1)S(1)}, bf16[16,32,2,128]{3,1,2,0:T(8,128)(2,1)S(1)}, u32[]{:S(2)}, u32[]{:S(2)}) collective-permute-start(bf16[16,32,2,128]{3,1,2,0:T(8,128)(2,1)S(1)} %bitcast.338), channel_id=1, source_target_pairs={{0,1},{1,2},{2,3},{4,5},{5,6},{6,7},{8,9},{9,10},{10,11},{12,13},{... | collective-permute-start | bytes 786440 | tf_op jit(solution)/shard_map/ppermute | solution.py:13
  53.0 0.8 multiply_reduce_fusion
  53.8 2.8 %stack.127 = f32[32,25]{0,1:T(8,128)S(1)} concatenate(f32[32,1]{0,1:T(1,128)} %bitcast.361, f32[32,1]{0,1:T(1,128)} %bitcast.359, f32[32,1]{0,1:T(1,128)} %bitcast.362, f32[32,1]{0,1:T(1,128)} %bitcast.358, f32[32,1]{0,1:T(1,128)} %bitcast.357, f32[32,1]{0,1:T(1,128)} %bitcast.356, f32[32,1]{0,1:T(1,128)} %bitcast.355, f32[32,1]{0,1:T(1,128)} %bitcast.363, f32[32,1]{0,1:T(1,128)} %bitcast.354, ...), dimensions={1} | concatenate | bytes 6400 | tf_op jit(solution)/shard_map/stack | solution.py:137
  56.6 3.7 %collective-permute-done.3 = bf16[16,32,256]{2,1,0:T(8,128)(2,1)} collective-permute-done((bf16[16,32,256]{2,1,0:T(8,128)(2,1)S(1)}, bf16[16,32,256]{2,1,0:T(8,128)(2,1)}, u32[]{:S(2)}, u32[]{:S(2)}) %collective-permute-start.3) | collective-permute-done | bytes 262176 | tf_op jit(solution)/shard_map/ppermute | solution.py:24
  60.3 1.3 fusion.21
  61.6 1.3 fusion.20
  63.0 1.3 fusion.19
  64.5 1.3 fusion.17
  65.8 1.3 fusion.16
  67.1 1.3 fusion.15
  68.4 59.4 %all-reduce.14 = (f32[32,25]{0,1:T(8,128)S(1)}, f32[32,32]{1,0:T(8,128)S(1)}, f32[7,32,32]{2,1,0:T(8,128)S(1)}) all-reduce(f32[32,25]{0,1:T(8,128)S(1)} %stack.127, f32[32,32]{1,0:T(8,128)S(1)} %convolution_bitcast_fusion.8, f32[7,32,32]{2,1,0:T(8,128)S(1)} %fusion.15), channel_id=1, replica_groups=mesh['grp'=2,'chan'=4,'tile'=2,'sub'=2] {'chan','tile','sub'}, use_global_device_ids=true, to_apply=%region_1.2 | all-reduce | flops 8992 | bytes 71936 | tf_op jit(solution)/shard_map/psum | solution.py:139
  127.8 0.7 broadcast_multiply_fusion
  128.5 1.3 fusion.130
  129.8 1.3 fusion.136
  131.1 1.3 fusion.139
  132.4 1.3 fusion.133
  133.7 1.3 convolution_add_fusion.1
  135.0 1.3 fusion.14
  136.3 0.6 broadcast_multiply_fusion.1
  137.8 0.7 copy.44
  138.5 1.0 add_convert_fusion
  139.5 0.7 fusion.1
  140.3 3.0 %fusion.49 = bf16[16,32,2,128]{3,1,2,0:T(8,128)(2,1)S(1)} fusion(f32[16,32,6,132]{3,1,2,0:T(8,128)S(1)} %fusion.1, bf16[16,32,2,128]{3,2,1,0:T(2,128)(2,1)S(1)} %copy-done.2, f32[32]{0:T(128)S(1)} %get-tuple-element.66, f32[32]{0:T(128)S(1)} %get-tuple-element.67, f32[32]{0:T(128)S(1)} %get-tuple-element.44, f32[32]{0:T(128)S(1)} %get-tuple-element.45, ...), kind=kLoop, calls=%fused_computation.100 | loop fusion | flops 6815744 | bytes 13634688 | tf_op jit(solution)/shard_map/convert_element_type | solution.py:138
  143.3 0.9 copy.43
  (73 shorter events, 4.7 us)
Async XLA Ops:
  0.6 31.8 %copy-start = (bf16[32,32]{1,0:T(8,128)(2,1)S(1)}, bf16[32,32]{1,0:T(8,128)(2,1)}, u32[]{:S(2)}) copy-start(bf16[32,32]{1,0:T(8,128)(2,1)} %param.9) | copy-start | bytes 6148
  0.6 21.9 %copy-start.8 = (bf16[7,32,32]{2,1,0:T(8,128)(2,1)S(1)}, bf16[7,32,32]{2,1,0:T(8,128)(2,1)}, u32[]{:S(2)}) copy-start(bf16[7,32,32]{2,1,0:T(8,128)(2,1)} %param.10) | copy-start | bytes 43012
  3.8 17.8 %collective-permute-start.7 = (bf16[16,32,256]{2,1,0:T(8,128)(2,1)S(1)}, bf16[16,32,256]{2,1,0:T(8,128)(2,1)S(1)}, u32[]{:S(2)}, u32[]{:S(2)}) collective-permute-start(bf16[16,32,256]{2,1,0:T(8,128)(2,1)S(1)} %gather_fusion.2), channel_id=1, source_target_pairs={{8,0},{12,4},{0,8},{4,12},{9,1},{13,5},{1,9},{5,13},{10,2},{14,6},... | collective-permute-start | bytes 786440 | tf_op jit(solution)/shard_map/ppermute | solution.py:24
  7.9 19.0 %collective-permute-start.6 = (bf16[16,32,256]{2,1,0:T(8,128)(2,1)S(1)}, bf16[16,32,256]{2,1,0:T(8,128)(2,1)S(1)}, u32[]{:S(2)}, u32[]{:S(2)}) collective-permute-start(bf16[16,32,256]{2,1,0:T(8,128)(2,1)S(1)} %gather_fusion.2), channel_id=1, source_target_pairs={{4,0},{8,4},{12,8},{0,12},{5,1},{9,5},{13,9},{1,13},{6,2},{10,6},{... | collective-permute-start | bytes 786440 | tf_op jit(solution)/shard_map/ppermute | solution.py:24
  9.2 17.4 %collective-permute-start.5 = (bf16[16,32,256]{2,1,0:T(8,128)(2,1)S(1)}, bf16[16,32,256]{2,1,0:T(8,128)(2,1)S(1)}, u32[]{:S(2)}, u32[]{:S(2)}) collective-permute-start(bf16[16,32,256]{2,1,0:T(8,128)(2,1)S(1)} %gather_fusion.2), channel_id=1, source_target_pairs={{12,0},{0,4},{4,8},{8,12},{13,1},{1,5},{5,9},{9,13},{14,2},{2,6},{... | collective-permute-start | bytes 786440 | tf_op jit(solution)/shard_map/ppermute | solution.py:24
  10.9 17.6 %copy-start.3 = (bf16[16,32,2,128]{3,1,2,0:T(8,128)(2,1)}, bf16[16,32,2,128]{3,1,2,0:T(8,128)(2,1)S(1)}, u32[]{:S(2)}) copy-start(bf16[16,32,2,128]{3,1,2,0:T(8,128)(2,1)S(1)} %copy.27) | copy-start | bytes 786436
  10.9 17.6 %collective-permute-start.1 = (bf16[16,32,2,128]{3,1,2,0:T(8,128)(2,1)S(1)}, bf16[16,32,2,128]{3,1,2,0:T(8,128)(2,1)S(1)}, u32[]{:S(2)}, u32[]{:S(2)}) collective-permute-start(bf16[16,32,2,128]{3,1,2,0:T(8,128)(2,1)S(1)} %copy.27), channel_id=1, source_target_pairs={{1,0},{2,1},{3,2},{5,4},{6,5},{7,6},{9,8},{10,9},{11,10},{13,12},{... | collective-permute-start | bytes 786440 | tf_op jit(solution)/shard_map/ppermute | solution.py:16
  12.2 16.3 %collective-permute-start = (bf16[16,32,2,128]{3,1,2,0:T(8,128)(2,1)S(1)}, bf16[16,32,2,128]{3,1,2,0:T(8,128)(2,1)S(1)}, u32[]{:S(2)}, u32[]{:S(2)}) collective-permute-start(bf16[16,32,2,128]{3,1,2,0:T(8,128)(2,1)S(1)} %copy.27), channel_id=1, source_target_pairs={{0,1},{1,2},{2,3},{4,5},{5,6},{6,7},{8,9},{9,10},{10,11},{12,13},{... | collective-permute-start | bytes 786440 | tf_op jit(solution)/shard_map/ppermute | solution.py:13
  27.8 1.5 %copy-start.9 = (f32[32]{0:T(128)S(1)}, f32[32]{0:T(128)}, u32[]{:S(2)}) copy-start(f32[32]{0:T(128)} %get-tuple-element.55) | copy-start | bytes 388
  27.8 1.5 %copy-start.11 = (f32[32]{0:T(128)S(1)}, f32[32]{0:T(128)}, u32[]{:S(2)}) copy-start(f32[32]{0:T(128)} %get-tuple-element.56) | copy-start | bytes 388
  27.8 1.5 %copy-start.13 = (f32[32]{0:T(128)S(1)}, f32[32]{0:T(128)}, u32[]{:S(2)}) copy-start(f32[32]{0:T(128)} %get-tuple-element.57) | copy-start | bytes 388
  27.8 1.5 %copy-start.15 = (f32[32]{0:T(128)S(1)}, f32[32]{0:T(128)}, u32[]{:S(2)}) copy-start(f32[32]{0:T(128)} %get-tuple-element.58) | copy-start | bytes 388
  27.9 1.5 %copy-start.17 = (f32[32]{0:T(128)S(1)}, f32[32]{0:T(128)}, u32[]{:S(2)}) copy-start(f32[32]{0:T(128)} %get-tuple-element.59) | copy-start | bytes 388
  27.9 1.5 %copy-start.19 = (f32[32]{0:T(128)S(1)}, f32[32]{0:T(128)}, u32[]{:S(2)}) copy-start(f32[32]{0:T(128)} %get-tuple-element.60) | copy-start | bytes 388
  27.9 1.5 %copy-start.21 = (f32[32]{0:T(128)S(1)}, f32[32]{0:T(128)}, u32[]{:S(2)}) copy-start(f32[32]{0:T(128)} %get-tuple-element.61) | copy-start | bytes 388
  28.5 3.9 %copy-start.6 = (bf16[16,32,2,128]{3,1,2,0:T(8,128)(2,1)}, bf16[16,32,2,128]{3,1,2,0:T(8,128)(2,1)S(1)}, u32[]{:S(2)}) copy-start(bf16[16,32,2,128]{3,1,2,0:T(8,128)(2,1)S(1)} %collective-permute-done.1) | copy-start | bytes 786436
  28.5 0.8 copy-start.7
  32.4 11.1 %copy-start.4 = (bf16[16,32,2,128]{3,1,2,0:T(8,128)(2,1)S(1)}, bf16[16,32,2,128]{3,1,2,0:T(8,128)(2,1)}, u32[]{:S(2)}) copy-start(bf16[16,32,2,128]{3,1,2,0:T(8,128)(2,1)} %copy-done.3) | copy-start | bytes 786436
  34.2 27.5 %collective-permute-start.4 = (bf16[16,32,256]{2,1,0:T(8,128)(2,1)S(1)}, bf16[16,32,256]{2,1,0:T(8,128)(2,1)}, u32[]{:S(2)}, u32[]{:S(2)}) collective-permute-start(bf16[16,32,256]{2,1,0:T(8,128)(2,1)S(1)} %gather_fusion), channel_id=1, source_target_pairs={{8,0},{12,4},{0,8},{4,12},{9,1},{13,5},{1,9},{5,13},{10,2},{14,6},... | collective-permute-start | bytes 786440 | tf_op jit(solution)/shard_map/ppermute | solution.py:24
  41.3 19.0 %collective-permute-start.3 = (bf16[16,32,256]{2,1,0:T(8,128)(2,1)S(1)}, bf16[16,32,256]{2,1,0:T(8,128)(2,1)}, u32[]{:S(2)}, u32[]{:S(2)}) collective-permute-start(bf16[16,32,256]{2,1,0:T(8,128)(2,1)S(1)} %gather_fusion), channel_id=1, source_target_pairs={{4,0},{8,4},{12,8},{0,12},{5,1},{9,5},{13,9},{1,13},{6,2},{10,6},{... | collective-permute-start | bytes 786440 | tf_op jit(solution)/shard_map/ppermute | solution.py:24
  41.8 21.2 %collective-permute-start.2 = (bf16[16,32,256]{2,1,0:T(8,128)(2,1)S(1)}, bf16[16,32,256]{2,1,0:T(8,128)(2,1)}, u32[]{:S(2)}, u32[]{:S(2)}) collective-permute-start(bf16[16,32,256]{2,1,0:T(8,128)(2,1)S(1)} %gather_fusion), channel_id=1, source_target_pairs={{12,0},{0,4},{4,8},{8,12},{13,1},{1,5},{5,9},{9,13},{14,2},{2,6},{... | collective-permute-start | bytes 786440 | tf_op jit(solution)/shard_map/ppermute | solution.py:24
  46.0 6.8 %copy-start.5 = (bf16[16,32,2,128]{3,1,2,0:T(8,128)(2,1)S(1)}, bf16[16,32,2,128]{3,1,2,0:T(8,128)(2,1)}, u32[]{:S(2)}) copy-start(bf16[16,32,2,128]{3,1,2,0:T(8,128)(2,1)} %get-tuple-element.73) | copy-start | bytes 786436
  46.0 7.0 %copy-start.1 = (bf16[16,32,2,128]{3,2,1,0:T(2,128)(2,1)S(1)}, bf16[16,32,2,128]{3,2,1,0:T(2,128)(2,1)}, u32[]{:S(2)}) copy-start(bf16[16,32,2,128]{3,2,1,0:T(2,128)(2,1)} %param.6) | copy-start | bytes 786436
  48.4 91.1 %collective-permute-start.9 = (bf16[16,32,2,128]{3,1,2,0:T(8,128)(2,1)S(1)}, bf16[16,32,2,128]{3,1,2,0:T(8,128)(2,1)S(1)}, u32[]{:S(2)}, u32[]{:S(2)}) collective-permute-start(bf16[16,32,2,128]{3,1,2,0:T(8,128)(2,1)S(1)} %bitcast.337), channel_id=1, source_target_pairs={{1,0},{2,1},{3,2},{5,4},{6,5},{7,6},{9,8},{10,9},{11,10},{13,12},{... | collective-permute-start | bytes 786440 | tf_op jit(solution)/shard_map/ppermute | solution.py:16
  49.7 89.8 %collective-permute-start.8 = (bf16[16,32,2,128]{3,1,2,0:T(8,128)(2,1)S(1)}, bf16[16,32,2,128]{3,1,2,0:T(8,128)(2,1)S(1)}, u32[]{:S(2)}, u32[]{:S(2)}) collective-permute-start(bf16[16,32,2,128]{3,1,2,0:T(8,128)(2,1)S(1)} %bitcast.338), channel_id=1, source_target_pairs={{0,1},{1,2},{2,3},{4,5},{5,6},{6,7},{8,9},{9,10},{10,11},{12,13},{... | collective-permute-start | bytes 786440 | tf_op jit(solution)/shard_map/ppermute | solution.py:13
  136.9 3.3 %copy-start.2 = (bf16[16,32,2,128]{3,2,1,0:T(2,128)(2,1)S(1)}, bf16[16,32,2,128]{3,2,1,0:T(2,128)(2,1)}, u32[]{:S(2)}) copy-start(bf16[16,32,2,128]{3,2,1,0:T(2,128)(2,1)} %param.7) | copy-start | bytes 786436
  136.9 3.3 %copy-start.10 = (f32[32]{0:T(128)S(1)}, f32[32]{0:T(128)}, u32[]{:S(2)}) copy-start(f32[32]{0:T(128)} %get-tuple-element.55) | copy-start | bytes 388
  136.9 3.3 %copy-start.12 = (f32[32]{0:T(128)S(1)}, f32[32]{0:T(128)}, u32[]{:S(2)}) copy-start(f32[32]{0:T(128)} %get-tuple-element.56) | copy-start | bytes 388
  136.9 3.3 %copy-start.14 = (f32[32]{0:T(128)S(1)}, f32[32]{0:T(128)}, u32[]{:S(2)}) copy-start(f32[32]{0:T(128)} %get-tuple-element.57) | copy-start | bytes 388
  136.9 3.3 %copy-start.16 = (f32[32]{0:T(128)S(1)}, f32[32]{0:T(128)}, u32[]{:S(2)}) copy-start(f32[32]{0:T(128)} %get-tuple-element.58) | copy-start | bytes 388
  136.9 3.3 %copy-start.18 = (f32[32]{0:T(128)S(1)}, f32[32]{0:T(128)}, u32[]{:S(2)}) copy-start(f32[32]{0:T(128)} %get-tuple-element.59) | copy-start | bytes 388
  136.9 3.3 %copy-start.20 = (f32[32]{0:T(128)S(1)}, f32[32]{0:T(128)}, u32[]{:S(2)}) copy-start(f32[32]{0:T(128)} %get-tuple-element.60) | copy-start | bytes 388
  137.0 3.3 %copy-start.22 = (f32[32]{0:T(128)S(1)}, f32[32]{0:T(128)}, u32[]{:S(2)}) copy-start(f32[32]{0:T(128)} %get-tuple-element.61) | copy-start | bytes 388
where the time goes:
time: 145 us; the launch traced here: 144 us
  blocking collectives  59.4 us (41%)
  starting transfers between devices  24 us (17%)
  matrix products  23.1 us (16%)
  other arithmetic  13.7 us (9%)
  local copies, waits for them, and re-layouts  13.6 us (9%)
  waiting for transfers between devices  9.18 us (6%)
    psum x1, blocking collectives, local(): lax.psum((kernel_term, mix_term, spec_grad), ('chan', 'tile', 'sub'))  59.4 us
    ppermute x6, starting transfers between devices, passed_along(): return lax.ppermute(block, axis, route)  15.3 us
    ppermute x6, waiting for transfers between devices, passed_along(): return lax.ppermute(block, axis, route)  9.17 us
    dot_general x6, matrix products, local(): jnp.einsum('gf,mfp->mgp', spectral_kernel[half + offset], h_near, preferr...  7.81 us
    dot_general x6, matrix products, local(): jnp.einsum('mgp,mfp->gf', g_sorted, h_near, preferred_element_type=jnp.fl...  7.77 us
    ppermute x2, starting transfers between devices, padded(): lax.ppermute(lax.slice_in_dim(block, block.shape[dim] - width, None, axis...  6.09 us
    slice x2, local copies, waits for them, and re-layouts, local(): spatial_kernel[:, i * 5 + j][None, :, None, None]  3.76 us
    dot_general x2, other arithmetic, local(): jnp.einsum('cfhw,cfhw->f', dsmooth, xpad[:, :, i:i + rows, j:j + cols], p...  3.12 us
  transfers between devices with their start and end apart: 10, of which 3 were waited for; matrix products, arithmetic and copies ran while one was open for 26% of the time, Pallas kernels for 0%

commit v1 on v0

--- a/solution.py
+++ b/solution.py
@@ -1,8 +1,18 @@
+import functools
 import math
 import jax
 import jax.numpy as jnp
 from jax import lax
 from jax.sharding import PartitionSpec as P
+
+
+def area_order(array_here, shard_axis, mesh_ax):
+    for c in (shard_axis, mesh_ax):
+        array_here = lax.psum(array_here, axis_name=c)
+    return array_here
+
+
+fix_the_scenes = functools.partial(area_order, shard_axis=("tile", "sub"), mesh_ax="chan")
 
 
 def padded(block, sides, width):
@@ -136,7 +146,7 @@
             )
     kernel_term = jnp.stack(terms, 1)
     dirty_grad = (cotangent.astype(jnp.float32) + conv).astype(jnp.bfloat16)
-    kgrad, mgrad, sgrad = lax.psum((kernel_term, mix_term, spec_grad), ("chan", "tile", "sub"))
+    kgrad, mgrad, sgrad = fix_the_scenes((kernel_term, mix_term, spec_grad))
     return (restored, dirty_grad, kgrad * scale, mgrad * scale, sgrad * scale)
 
 

time: 145 us -> 122 us (0.84)
  blocking collectives: 59.4 us -> 36.1 us
    psum x1 -> x2, blocking collectives: 59.4 us -> 36.1 us  [area_order(): array_here = lax.psum(array_here, axis_name=c)]
  transfers between devices with their start and end apart: 10 -> 10, of which waited for: 3 -> 3; matrix products, arithmetic and copies ran while one was open for 26% -> 31% of each run, Pallas kernels for 0% -> 0%
where the time goes in v1:
time: 122 us; the launch traced here: 121 us
  blocking collectives  36.1 us (30%)
  starting transfers between devices  24 us (20%)
  matrix products  23.1 us (19%)
  other arithmetic  13.7 us (11%)
  local copies, waits for them, and re-layouts  13.6 us (11%)
  waiting for transfers between devices  9.18 us (8%)
  between operations  1.26 us (1%)
    psum x2, blocking collectives, area_order(): array_here = lax.psum(array_here, axis_name=c)  36.1 us
    ppermute x6, starting transfers between devices, passed_along(): return lax.ppermute(block, axis, route)  15.3 us
    ppermute x6, waiting for transfers between devices, passed_along(): return lax.ppermute(block, axis, route)  9.17 us
    dot_general x6, matrix products, local(): jnp.einsum('gf,mfp->mgp', spectral_kernel[half + offset], h_near, preferr...  7.81 us
    dot_general x6, matrix products, local(): jnp.einsum('mgp,mfp->gf', g_sorted, h_near, preferred_element_type=jnp.fl...  7.77 us
    ppermute x2, starting transfers between devices, padded(): lax.ppermute(lax.slice_in_dim(block, block.shape[dim] - width, None, axis...  6.09 us
    slice x2, local copies, waits for them, and re-layouts, local(): spatial_kernel[:, i * 5 + j][None, :, None, None]  3.76 us
    dot_general x2, other arithmetic, local(): jnp.einsum('cfhw,cfhw->f', dsmooth, xpad[:, :, i:i + rows, j:j + cols], p...  3.12 us
  transfers between devices with their start and end apart: 10, of which 3 were waited for; matrix products, arithmetic and copies ran while one was open for 31% of the time, Pallas kernels for 0%

profile of v1, /device:TPU:0, one launch (start us, length us, event | category | flops | bytes accessed | tf_op | source)
XLA Modules:
  0.0 120.9 jit_solution(2755329282119038684)
XLA Ops:
  0.7 0.8 compare_select_fusion.1
  1.4 0.6 scatter_custom_fusion
  2.1 1.1 reshape.48
  3.8 4.1 %collective-permute-start.7 = (bf16[16,32,256]{2,1,0:T(8,128)(2,1)S(1)}, bf16[16,32,256]{2,1,0:T(8,128)(2,1)S(1)}, u32[]{:S(2)}, u32[]{:S(2)}) collective-permute-start(bf16[16,32,256]{2,1,0:T(8,128)(2,1)S(1)} %gather_fusion.2), channel_id=1, source_target_pairs={{8,0},{12,4},{0,8},{4,12},{9,1},{13,5},{1,9},{5,13},{10,2},{14,6},... | collective-permute-start | bytes 786440 | tf_op jit(solution)/shard_map/ppermute | solution.py:34
  7.9 1.3 %collective-permute-start.6 = (bf16[16,32,256]{2,1,0:T(8,128)(2,1)S(1)}, bf16[16,32,256]{2,1,0:T(8,128)(2,1)S(1)}, u32[]{:S(2)}, u32[]{:S(2)}) collective-permute-start(bf16[16,32,256]{2,1,0:T(8,128)(2,1)S(1)} %gather_fusion.2), channel_id=1, source_target_pairs={{4,0},{8,4},{12,8},{0,12},{5,1},{9,5},{13,9},{1,13},{6,2},{10,6},{... | collective-permute-start | bytes 786440 | tf_op jit(solution)/shard_map/ppermute | solution.py:34
  9.2 0.7 collective-permute-start.5
  9.9 1.0 copy.27
  10.9 1.3 %collective-permute-start.1 = (bf16[16,32,2,128]{3,1,2,0:T(8,128)(2,1)S(1)}, bf16[16,32,2,128]{3,1,2,0:T(8,128)(2,1)S(1)}, u32[]{:S(2)}, u32[]{:S(2)}) collective-permute-start(bf16[16,32,2,128]{3,1,2,0:T(8,128)(2,1)S(1)} %copy.27), channel_id=1, source_target_pairs={{1,0},{2,1},{3,2},{5,4},{6,5},{7,6},{9,8},{10,9},{11,10},{13,12},{... | collective-permute-start | bytes 786440 | tf_op jit(solution)/shard_map/ppermute | solution.py:26
  12.2 3.0 %collective-permute-start = (bf16[16,32,2,128]{3,1,2,0:T(8,128)(2,1)S(1)}, bf16[16,32,2,128]{3,1,2,0:T(8,128)(2,1)S(1)}, u32[]{:S(2)}, u32[]{:S(2)}) collective-permute-start(bf16[16,32,2,128]{3,1,2,0:T(8,128)(2,1)S(1)} %copy.27), channel_id=1, source_target_pairs={{0,1},{1,2},{2,3},{4,5},{5,6},{6,7},{8,9},{9,10},{10,11},{12,13},{... | collective-permute-start | bytes 786440 | tf_op jit(solution)/shard_map/ppermute | solution.py:23
  15.3 1.2 %slice_reduce_fusion.23 = (f32[32]{0:T(128)S(1)}, f32[32]{0:T(128)S(1)}, f32[32]{0:T(128)S(1)}, f32[32]{0:T(128)S(1)}, f32[32]{0:T(128)S(1)}, /*index=5*/f32[32]{0:T(128)S(1)}) fusion(f32[32,25]{1,0:T(8,128)} %param.8), kind=kLoop, calls=%fused_computation.292 | loop fusion | bytes 1536 | tf_op jit(solution)/shard_map/slice | solution.py:66
  16.5 2.5 %slice_reduce_fusion.24 = (f32[32]{0:T(128)S(1)}, f32[32]{0:T(128)S(1)}, f32[32]{0:T(128)S(1)}, f32[32]{0:T(128)S(1)}, f32[32]{0:T(128)S(1)}, /*index=5*/f32[32]...) fusion(f32[32,25]{1,0:T(8,128)} %param.8), kind=kLoop, calls=%fused_computation.293 | loop fusion | bytes 4864 | tf_op jit(solution)/shard_map/slice | solution.py:66
  19.0 1.0 fusion.159
  20.0 1.5 %collective-permute-done.7 = bf16[16,32,256]{2,1,0:T(8,128)(2,1)S(1)} collective-permute-done((bf16[16,32,256]{2,1,0:T(8,128)(2,1)S(1)}, bf16[16,32,256]{2,1,0:T(8,128)(2,1)S(1)}, u32[]{:S(2)}, u32[]{:S(2)}) %collective-permute-start.7) | collective-permute-done | bytes 262176 | tf_op jit(solution)/shard_map/ppermute | solution.py:34
  21.5 1.0 fusion.109
  22.8 3.9 %collective-permute-done.5 = bf16[16,32,256]{2,1,0:T(8,128)(2,1)S(1)} collective-permute-done((bf16[16,32,256]{2,1,0:T(8,128)(2,1)S(1)}, bf16[16,32,256]{2,1,0:T(8,128)(2,1)S(1)}, u32[]{:S(2)}, u32[]{:S(2)}) %collective-permute-start.5) | collective-permute-done | bytes 262176 | tf_op jit(solution)/shard_map/ppermute | solution.py:34
  28.5 0.8 select_maximum_fusion.2
  29.4 3.0 %fusion.74 = bf16[16,32,2,128]{3,1,2,0:T(8,128)(2,1)S(1)} fusion(f32[16,32,6,132]{3,1,2,0:T(8,128)S(1)} %get-tuple-element.75, f32[32]{0:T(128)S(1)} %get-tuple-element.66, f32[32]{0:T(128)S(1)} %get-tuple-element.67, f32[32]{0:T(128)S(1)} %get-tuple-element.44, f32[32]{0:T(128)S(1)} %get-tuple-element.45, f32[32]{0:T(128)S(1)} %get-tuple-element.46, ...), kind=kLoop, calls=%fused_computation.150 | loop fusion | flops 6553600 | bytes 13372544 | tf_op jit(solution)/shard_map/convert_element_type | solution.py:69
  32.4 1.1 fusion.46
  34.2 7.2 %collective-permute-start.4 = (bf16[16,32,256]{2,1,0:T(8,128)(2,1)S(1)}, bf16[16,32,256]{2,1,0:T(8,128)(2,1)}, u32[]{:S(2)}, u32[]{:S(2)}) collective-permute-start(bf16[16,32,256]{2,1,0:T(8,128)(2,1)S(1)} %gather_fusion), channel_id=1, source_target_pairs={{8,0},{12,4},{0,8},{4,12},{9,1},{13,5},{1,9},{5,13},{10,2},{14,6},... | collective-permute-start | bytes 786440 | tf_op jit(solution)/shard_map/ppermute | solution.py:34
  41.8 1.6 %collective-permute-start.2 = (bf16[16,32,256]{2,1,0:T(8,128)(2,1)S(1)}, bf16[16,32,256]{2,1,0:T(8,128)(2,1)}, u32[]{:S(2)}, u32[]{:S(2)}) collective-permute-start(bf16[16,32,256]{2,1,0:T(8,128)(2,1)S(1)} %gather_fusion), channel_id=1, source_target_pairs={{12,0},{0,4},{4,8},{8,12},{13,1},{1,5},{5,9},{9,13},{14,2},{2,6},{... | collective-permute-start | bytes 786440 | tf_op jit(solution)/shard_map/ppermute | solution.py:34
  43.6 2.5 %fusion.44 = (f32[32]{0:T(128)}, f32[32]{0:T(128)}, f32[32]{0:T(128)}, f32[32]{0:T(128)}, f32[32]{0:T(128)}, /*index=5*/f32[32]{0:T(128)}, bf16[16,2,128,32]{2,3,1,0:T(8,128)(2,1)S(1)}) fusion(bf16[16,32,6,132]{3,1,2,0:T(8,128)(2,1)S(1)} %get-tuple-element.74, bf16[16,32,2,128]{3,1,2,0:T(8,128)(2,1)} %copy-done.7, ...), kind=kOutput, calls=%fused_computation.93 | convolution fusion | flops 11272000 | bytes 1837824 | tf_op jit(solution)/shard_map/gf,cghw->cfhw/dot_general | solution.py:125
  46.0 2.3 %fusion.45 = (f32[32]{0:T(128)}, f32[32]{0:T(128)}, f32[32]{0:T(128)}, f32[32]{0:T(128)}, f32[32]{0:T(128)}, /*index=5*/f32[32]{0:T(128)}, f32[32]{0:T(128)}, f3...) fusion(bf16[16,32,6,132]{3,1,2,0:T(8,128)(2,1)S(1)} %get-tuple-, ...), kind=kLoop, calls=%fused_computation.94 | loop fusion | flops 7208384 | bytes 4983040 | tf_op jit(solution)/shard_map/cfhw,cfhw->f/dot_general | solution.py:140
  48.4 1.3 %collective-permute-start.9 = (bf16[16,32,2,128]{3,1,2,0:T(8,128)(2,1)S(1)}, bf16[16,32,2,128]{3,1,2,0:T(8,128)(2,1)S(1)}, u32[]{:S(2)}, u32[]{:S(2)}) collective-permute-start(bf16[16,32,2,128]{3,1,2,0:T(8,128)(2,1)S(1)} %bitcast.337), channel_id=1, source_target_pairs={{1,0},{2,1},{3,2},{5,4},{6,5},{7,6},{9,8},{10,9},{11,10},{13,12},{... | collective-permute-start | bytes 786440 | tf_op jit(solution)/shard_map/ppermute | solution.py:26
  49.7 3.0 %collective-permute-start.8 = (bf16[16,32,2,128]{3,1,2,0:T(8,128)(2,1)S(1)}, bf16[16,32,2,128]{3,1,2,0:T(8,128)(2,1)S(1)}, u32[]{:S(2)}, u32[]{:S(2)}) collective-permute-start(bf16[16,32,2,128]{3,1,2,0:T(8,128)(2,1)S(1)} %bitcast.338), channel_id=1, source_target_pairs={{0,1},{1,2},{2,3},{4,5},{5,6},{6,7},{8,9},{9,10},{10,11},{12,13},{... | collective-permute-start | bytes 786440 | tf_op jit(solution)/shard_map/ppermute | solution.py:23
  53.0 0.8 multiply_reduce_fusion
  53.8 2.8 %stack.127 = f32[32,25]{0,1:T(8,128)S(1)} concatenate(f32[32,1]{0,1:T(1,128)} %bitcast.361, f32[32,1]{0,1:T(1,128)} %bitcast.359, f32[32,1]{0,1:T(1,128)} %bitcast.362, f32[32,1]{0,1:T(1,128)} %bitcast.358, f32[32,1]{0,1:T(1,128)} %bitcast.357, f32[32,1]{0,1:T(1,128)} %bitcast.356, f32[32,1]{0,1:T(1,128)} %bitcast.355, f32[32,1]{0,1:T(1,128)} %bitcast.363, f32[32,1]{0,1:T(1,128)} %bitcast.354, ...), dimensions={1} | concatenate | bytes 6400 | tf_op jit(solution)/shard_map/stack | solution.py:147
  56.6 3.7 %collective-permute-done.3 = bf16[16,32,256]{2,1,0:T(8,128)(2,1)} collective-permute-done((bf16[16,32,256]{2,1,0:T(8,128)(2,1)S(1)}, bf16[16,32,256]{2,1,0:T(8,128)(2,1)}, u32[]{:S(2)}, u32[]{:S(2)}) %collective-permute-start.3) | collective-permute-done | bytes 262176 | tf_op jit(solution)/shard_map/ppermute | solution.py:34
  60.3 1.3 %fusion.21 = f32[7,32,32]{2,1,0:T(8,128)S(1)} fusion(bf16[16,32,256]{2,1,0:T(8,128)(2,1)S(1)} %gather_fusion.2, bf16[16,32,256]{2,1,0:T(8,128)(2,1)} %collective-permute-done.3, pred[]{:T(512)S(6)} %lt.26), kind=kOutput, calls=%fused_computation.69 | convolution fusion | flops 8519679 | bytes 540673 | tf_op jit(solution)/shard_map/mgp,mfp->gf/dot_general | solution.py:114
  61.6 1.3 %fusion.20 = f32[7,32,32]{2,1,0:T(8,128)S(1)} fusion(f32[7,32,32]{2,1,0:T(8,128)S(1)} %fusion.21, bf16[16,32,256]{2,1,0:T(8,128)(2,1)S(1)} %gather_fusion.2, bf16[16,32,256]{2,1,0:T(8,128)(2,1)} %collective-permute-done.4, pred[]{:T(512)S(6)} %lt.25), kind=kOutput, calls=%fused_computation.67 | convolution fusion | flops 8519680 | bytes 540673 | tf_op jit(solution)/shard_map/mgp,mfp->gf/dot_general | solution.py:114
  63.0 1.3 %fusion.19 = f32[7,32,32]{2,1,0:T(8,128)S(1)} fusion(f32[7,32,32]{2,1,0:T(8,128)S(1)} %fusion.20, bf16[16,32,256]{2,1,0:T(8,128)(2,1)S(1)} %gather_fusion.2, bf16[16,32,256]{2,1,0:T(8,128)(2,1)} %collective-permute-done.2, pred[]{:T(512)S(6)} %lt.24), kind=kOutput, calls=%fused_computation.65 | convolution fusion | flops 8519680 | bytes 540673 | tf_op jit(solution)/shard_map/mgp,mfp->gf/dot_general | solution.py:114
  64.5 1.3 %fusion.17 = f32[7,32,32]{2,1,0:T(8,128)S(1)} fusion(f32[7,32,32]{2,1,0:T(8,128)S(1)} %fusion.18, bf16[16,32,256]{2,1,0:T(8,128)(2,1)S(1)} %gather_fusion.2, bf16[16,32,256]{2,1,0:T(8,128)(2,1)} %collective-permute-done.3, pred[]{:T(512)S(6)} %ge.9), kind=kOutput, calls=%fused_computation.61 | convolution fusion | flops 8519680 | bytes 540673 | tf_op jit(solution)/shard_map/mgp,mfp->gf/dot_general | solution.py:114
  65.8 1.3 %fusion.16 = f32[7,32,32]{2,1,0:T(8,128)S(1)} fusion(f32[7,32,32]{2,1,0:T(8,128)S(1)} %fusion.17, bf16[16,32,256]{2,1,0:T(8,128)(2,1)S(1)} %gather_fusion.2, bf16[16,32,256]{2,1,0:T(8,128)(2,1)} %collective-permute-done.4, pred[]{:T(512)S(6)} %ge.10), kind=kOutput, calls=%fused_computation.59 | convolution fusion | flops 8519680 | bytes 540673 | tf_op jit(solution)/shard_map/mgp,mfp->gf/dot_general | solution.py:114
  67.1 1.3 %fusion.15 = f32[7,32,32]{2,1,0:T(8,128)S(1)} fusion(f32[7,32,32]{2,1,0:T(8,128)S(1)} %fusion.16, bf16[16,32,256]{2,1,0:T(8,128)(2,1)S(1)} %gather_fusion.2, bf16[16,32,256]{2,1,0:T(8,128)(2,1)} %collective-permute-done.2, pred[]{:T(512)S(6)} %ge.11), kind=kOutput, calls=%fused_computation.57 | convolution fusion | flops 8519680 | bytes 540673 | tf_op jit(solution)/shard_map/mgp,mfp->gf/dot_general | solution.py:114
  68.4 11.6 %all-reduce.14 = (f32[32,25]{0,1:T(8,128)S(1)}, f32[32,32]{1,0:T(8,128)S(1)}, f32[7,32,32]{2,1,0:T(8,128)S(1)}) all-reduce(f32[32,25]{0,1:T(8,128)S(1)} %stack.127, f32[32,32]{1,0:T(8,128)S(1)} %convolution_bitcast_fusion.8, f32[7,32,32]{2,1,0:T(8,128)S(1)} %fusion.15), channel_id=1, replica_groups=mesh['grp'=2,'chan'=4,'tile'=2,'sub'=2] {'tile','sub'}, use_global_device_ids=true, to_apply=%region_1.2 | all-reduce | flops 8992 | bytes 71936 | tf_op jit(solution)/shard_map/psum | solution.py:11
  79.9 24.5 %all-reduce.15 = (f32[32,25]{0,1:T(8,128)S(1)}, f32[32,32]{1,0:T(8,128)S(1)}, f32[7,32,32]{2,1,0:T(8,128)S(1)}) all-reduce(f32[32,25]{0,1:T(8,128)S(1)} %get-tuple-element.68, f32[32,32]{1,0:T(8,128)S(1)} %get-tuple-element.69, f32[7,32,32]{2,1,0:T(8,128)S(1)} %get-tuple-element.70), channel_id=1, replica_groups=mesh['grp'=2,'chan'=4,'tile'=2,'sub'=2] {'chan'}, use_global_device_ids=true, to_apply=%region_2.3 | all-reduce | flops 8992 | bytes 71936 | tf_op jit(solution)/shard_map/psum | solution.py:11
  104.5 0.7 broadcast_multiply_fusion
  105.1 1.3 %fusion.130 = f32[16,256,32]{1,2,0:T(8,128)S(1)} fusion(bf16[16,32,256]{2,1,0:T(8,128)(2,1)} %collective-permute-done.2, pred[]{:T(512)S(6)} %ge.11, bf16[7,32,32]{2,1,0:T(8,128)(2,1)S(1)} %copy-done.8), kind=kOutput, calls=%fused_computation.265 | convolution fusion | flops 8519680 | bytes 794625 | tf_op jit(solution)/shard_map/gf,mfp->mgp/dot_general | solution.py:102
  106.4 1.3 %fusion.136 = f32[16,256,32]{1,2,0:T(8,128)S(1)} fusion(bf16[16,32,256]{2,1,0:T(8,128)(2,1)} %collective-permute-done.4, pred[]{:T(512)S(6)} %ge.10, bf16[7,32,32]{2,1,0:T(8,128)(2,1)S(1)} %copy-done.8), kind=kOutput, calls=%fused_computation.267 | convolution fusion | flops 8519680 | bytes 794625 | tf_op jit(solution)/shard_map/gf,mfp->mgp/dot_general | solution.py:102
  107.7 1.3 %fusion.139 = f32[16,256,32]{1,2,0:T(8,128)S(1)} fusion(bf16[16,32,256]{2,1,0:T(8,128)(2,1)} %collective-permute-done.4, pred[]{:T(512)S(6)} %lt.25, bf16[7,32,32]{2,1,0:T(8,128)(2,1)S(1)} %copy-done.8), kind=kOutput, calls=%fused_computation.268 | convolution fusion | flops 8519680 | bytes 794625 | tf_op jit(solution)/shard_map/gf,mfp->mgp/dot_general | solution.py:102
  109.0 1.3 %fusion.133 = f32[16,256,32]{1,2,0:T(8,128)S(1)} fusion(bf16[16,32,256]{2,1,0:T(8,128)(2,1)} %collective-permute-done.3, pred[]{:T(512)S(6)} %lt.26, bf16[7,32,32]{2,1,0:T(8,128)(2,1)S(1)} %copy-done.8), kind=kOutput, calls=%fused_computation.266 | convolution fusion | flops 8519680 | bytes 794625 | tf_op jit(solution)/shard_map/gf,mfp->mgp/dot_general | solution.py:102
  110.3 1.3 %convolution_add_fusion.1 = f32[16,256,32]{1,2,0:T(8,128)S(1)} fusion(f32[16,256,32]{1,2,0:T(8,128)S(1)} %fusion.161, bf16[16,32,256]{2,1,0:T(8,128)(2,1)} %collective-permute-done.2, pred[]{:T(512)S(6)} %lt.24, bf16[7,32,32]{2,1,0:T(8,128)(2,1)S(1)} %copy-done.8), kind=kOutput, calls=%fused_computation.39 | convolution fusion | flops 8650752 | bytes 1318913 | tf_op jit(solution)/shard_map/gf,mfp->mgp/dot_general | solution.py:102
  111.6 1.3 %fusion.14 = bf16[16,32,256]{2,1,0:T(8,128)(2,1)S(1)} fusion(f32[16,256,32]{1,2,0:T(8,128)S(1)} %fusion.130, f32[16,256,32]{1,2,0:T(8,128)S(1)} %fusion.133, f32[16,256,32]{1,2,0:T(8,128)S(1)} %fusion.136, f32[16,256,32]{1,2,0:T(8,128)S(1)} %fusion.139, f32[16,256,32]{1,2,0:T(8,128)S(1)} %convolution_add_fusion.1, ...), kind=kOutput, calls=%fused_computation.55 | convolution fusion | flops 9306112 | bytes 3153921 | tf_op jit(solution)/shard_map/gf,mfp->mgp/dot_general | solution.py:102
  113.0 0.6 broadcast_multiply_fusion.1
  114.5 0.7 copy.44
  115.1 1.0 add_convert_fusion
  116.1 0.7 fusion.1
  116.9 3.0 %fusion.49 = bf16[16,32,2,128]{3,1,2,0:T(8,128)(2,1)S(1)} fusion(f32[16,32,6,132]{3,1,2,0:T(8,128)S(1)} %fusion.1, bf16[16,32,2,128]{3,2,1,0:T(2,128)(2,1)S(1)} %copy-done.2, f32[32]{0:T(128)S(1)} %get-tuple-element.66, f32[32]{0:T(128)S(1)} %get-tuple-element.67, f32[32]{0:T(128)S(1)} %get-tuple-element.44, f32[32]{0:T(128)S(1)} %get-tuple-element.45, ...), kind=kLoop, calls=%fused_computation.100 | loop fusion | flops 6815744 | bytes 13634688 | tf_op jit(solution)/shard_map/convert_element_type | solution.py:148
  120.0 0.9 copy.43
  (74 shorter events, 5.2 us)
Async XLA Ops:
  0.6 31.8 %copy-start = (bf16[32,32]{1,0:T(8,128)(2,1)S(1)}, bf16[32,32]{1,0:T(8,128)(2,1)}, u32[]{:S(2)}) copy-start(bf16[32,32]{1,0:T(8,128)(2,1)} %param.9) | copy-start | bytes 6148
  0.6 21.9 %copy-start.8 = (bf16[7,32,32]{2,1,0:T(8,128)(2,1)S(1)}, bf16[7,32,32]{2,1,0:T(8,128)(2,1)}, u32[]{:S(2)}) copy-start(bf16[7,32,32]{2,1,0:T(8,128)(2,1)} %param.10) | copy-start | bytes 43012
  3.8 17.8 %collective-permute-start.7 = (bf16[16,32,256]{2,1,0:T(8,128)(2,1)S(1)}, bf16[16,32,256]{2,1,0:T(8,128)(2,1)S(1)}, u32[]{:S(2)}, u32[]{:S(2)}) collective-permute-start(bf16[16,32,256]{2,1,0:T(8,128)(2,1)S(1)} %gather_fusion.2), channel_id=1, source_target_pairs={{8,0},{12,4},{0,8},{4,12},{9,1},{13,5},{1,9},{5,13},{10,2},{14,6},... | collective-permute-start | bytes 786440 | tf_op jit(solution)/shard_map/ppermute | solution.py:34
  7.9 19.0 %collective-permute-start.6 = (bf16[16,32,256]{2,1,0:T(8,128)(2,1)S(1)}, bf16[16,32,256]{2,1,0:T(8,128)(2,1)S(1)}, u32[]{:S(2)}, u32[]{:S(2)}) collective-permute-start(bf16[16,32,256]{2,1,0:T(8,128)(2,1)S(1)} %gather_fusion.2), channel_id=1, source_target_pairs={{4,0},{8,4},{12,8},{0,12},{5,1},{9,5},{13,9},{1,13},{6,2},{10,6},{... | collective-permute-start | bytes 786440 | tf_op jit(solution)/shard_map/ppermute | solution.py:34
  9.2 17.4 %collective-permute-start.5 = (bf16[16,32,256]{2,1,0:T(8,128)(2,1)S(1)}, bf16[16,32,256]{2,1,0:T(8,128)(2,1)S(1)}, u32[]{:S(2)}, u32[]{:S(2)}) collective-permute-start(bf16[16,32,256]{2,1,0:T(8,128)(2,1)S(1)} %gather_fusion.2), channel_id=1, source_target_pairs={{12,0},{0,4},{4,8},{8,12},{13,1},{1,5},{5,9},{9,13},{14,2},{2,6},{... | collective-permute-start | bytes 786440 | tf_op jit(solution)/shard_map/ppermute | solution.py:34
  10.9 17.6 %copy-start.3 = (bf16[16,32,2,128]{3,1,2,0:T(8,128)(2,1)}, bf16[16,32,2,128]{3,1,2,0:T(8,128)(2,1)S(1)}, u32[]{:S(2)}) copy-start(bf16[16,32,2,128]{3,1,2,0:T(8,128)(2,1)S(1)} %copy.27) | copy-start | bytes 786436
  10.9 17.6 %collective-permute-start.1 = (bf16[16,32,2,128]{3,1,2,0:T(8,128)(2,1)S(1)}, bf16[16,32,2,128]{3,1,2,0:T(8,128)(2,1)S(1)}, u32[]{:S(2)}, u32[]{:S(2)}) collective-permute-start(bf16[16,32,2,128]{3,1,2,0:T(8,128)(2,1)S(1)} %copy.27), channel_id=1, source_target_pairs={{1,0},{2,1},{3,2},{5,4},{6,5},{7,6},{9,8},{10,9},{11,10},{13,12},{... | collective-permute-start | bytes 786440 | tf_op jit(solution)/shard_map/ppermute | solution.py:26
  12.2 16.3 %collective-permute-start = (bf16[16,32,2,128]{3,1,2,0:T(8,128)(2,1)S(1)}, bf16[16,32,2,128]{3,1,2,0:T(8,128)(2,1)S(1)}, u32[]{:S(2)}, u32[]{:S(2)}) collective-permute-start(bf16[16,32,2,128]{3,1,2,0:T(8,128)(2,1)S(1)} %copy.27), channel_id=1, source_target_pairs={{0,1},{1,2},{2,3},{4,5},{5,6},{6,7},{8,9},{9,10},{10,11},{12,13},{... | collective-permute-start | bytes 786440 | tf_op jit(solution)/shard_map/ppermute | solution.py:23
  27.8 1.5 %copy-start.9 = (f32[32]{0:T(128)S(1)}, f32[32]{0:T(128)}, u32[]{:S(2)}) copy-start(f32[32]{0:T(128)} %get-tuple-element.55) | copy-start | bytes 388
  27.8 1.5 %copy-start.11 = (f32[32]{0:T(128)S(1)}, f32[32]{0:T(128)}, u32[]{:S(2)}) copy-start(f32[32]{0:T(128)} %get-tuple-element.56) | copy-start | bytes 388
  27.8 1.5 %copy-start.13 = (f32[32]{0:T(128)S(1)}, f32[32]{0:T(128)}, u32[]{:S(2)}) copy-start(f32[32]{0:T(128)} %get-tuple-element.57) | copy-start | bytes 388
  27.8 1.5 %copy-start.15 = (f32[32]{0:T(128)S(1)}, f32[32]{0:T(128)}, u32[]{:S(2)}) copy-start(f32[32]{0:T(128)} %get-tuple-element.58) | copy-start | bytes 388
  27.9 1.5 %copy-start.17 = (f32[32]{0:T(128)S(1)}, f32[32]{0:T(128)}, u32[]{:S(2)}) copy-start(f32[32]{0:T(128)} %get-tuple-element.59) | copy-start | bytes 388
  27.9 1.5 %copy-start.19 = (f32[32]{0:T(128)S(1)}, f32[32]{0:T(128)}, u32[]{:S(2)}) copy-start(f32[32]{0:T(128)} %get-tuple-element.60) | copy-start | bytes 388
  27.9 1.5 %copy-start.21 = (f32[32]{0:T(128)S(1)}, f32[32]{0:T(128)}, u32[]{:S(2)}) copy-start(f32[32]{0:T(128)} %get-tuple-element.61) | copy-start | bytes 388
  28.5 3.9 %copy-start.6 = (bf16[16,32,2,128]{3,1,2,0:T(8,128)(2,1)}, bf16[16,32,2,128]{3,1,2,0:T(8,128)(2,1)S(1)}, u32[]{:S(2)}) copy-start(bf16[16,32,2,128]{3,1,2,0:T(8,128)(2,1)S(1)} %collective-permute-done.1) | copy-start | bytes 786436
  28.5 0.8 copy-start.7
  32.4 11.1 %copy-start.4 = (bf16[16,32,2,128]{3,1,2,0:T(8,128)(2,1)S(1)}, bf16[16,32,2,128]{3,1,2,0:T(8,128)(2,1)}, u32[]{:S(2)}) copy-start(bf16[16,32,2,128]{3,1,2,0:T(8,128)(2,1)} %copy-done.3) | copy-start | bytes 786436
  34.2 27.5 %collective-permute-start.4 = (bf16[16,32,256]{2,1,0:T(8,128)(2,1)S(1)}, bf16[16,32,256]{2,1,0:T(8,128)(2,1)}, u32[]{:S(2)}, u32[]{:S(2)}) collective-permute-start(bf16[16,32,256]{2,1,0:T(8,128)(2,1)S(1)} %gather_fusion), channel_id=1, source_target_pairs={{8,0},{12,4},{0,8},{4,12},{9,1},{13,5},{1,9},{5,13},{10,2},{14,6},... | collective-permute-start | bytes 786440 | tf_op jit(solution)/shard_map/ppermute | solution.py:34
  41.3 19.0 %collective-permute-start.3 = (bf16[16,32,256]{2,1,0:T(8,128)(2,1)S(1)}, bf16[16,32,256]{2,1,0:T(8,128)(2,1)}, u32[]{:S(2)}, u32[]{:S(2)}) collective-permute-start(bf16[16,32,256]{2,1,0:T(8,128)(2,1)S(1)} %gather_fusion), channel_id=1, source_target_pairs={{4,0},{8,4},{12,8},{0,12},{5,1},{9,5},{13,9},{1,13},{6,2},{10,6},{... | collective-permute-start | bytes 786440 | tf_op jit(solution)/shard_map/ppermute | solution.py:34
  41.8 21.2 %collective-permute-start.2 = (bf16[16,32,256]{2,1,0:T(8,128)(2,1)S(1)}, bf16[16,32,256]{2,1,0:T(8,128)(2,1)}, u32[]{:S(2)}, u32[]{:S(2)}) collective-permute-start(bf16[16,32,256]{2,1,0:T(8,128)(2,1)S(1)} %gather_fusion), channel_id=1, source_target_pairs={{12,0},{0,4},{4,8},{8,12},{13,1},{1,5},{5,9},{9,13},{14,2},{2,6},{... | collective-permute-start | bytes 786440 | tf_op jit(solution)/shard_map/ppermute | solution.py:34
  46.0 6.8 %copy-start.5 = (bf16[16,32,2,128]{3,1,2,0:T(8,128)(2,1)S(1)}, bf16[16,32,2,128]{3,1,2,0:T(8,128)(2,1)}, u32[]{:S(2)}) copy-start(bf16[16,32,2,128]{3,1,2,0:T(8,128)(2,1)} %get-tuple-element.76) | copy-start | bytes 786436
  46.0 7.0 %copy-start.1 = (bf16[16,32,2,128]{3,2,1,0:T(2,128)(2,1)S(1)}, bf16[16,32,2,128]{3,2,1,0:T(2,128)(2,1)}, u32[]{:S(2)}) copy-start(bf16[16,32,2,128]{3,2,1,0:T(2,128)(2,1)} %param.6) | copy-start | bytes 786436
  48.4 67.7 %collective-permute-start.9 = (bf16[16,32,2,128]{3,1,2,0:T(8,128)(2,1)S(1)}, bf16[16,32,2,128]{3,1,2,0:T(8,128)(2,1)S(1)}, u32[]{:S(2)}, u32[]{:S(2)}) collective-permute-start(bf16[16,32,2,128]{3,1,2,0:T(8,128)(2,1)S(1)} %bitcast.337), channel_id=1, source_target_pairs={{1,0},{2,1},{3,2},{5,4},{6,5},{7,6},{9,8},{10,9},{11,10},{13,12},{... | collective-permute-start | bytes 786440 | tf_op jit(solution)/shard_map/ppermute | solution.py:26
  49.7 66.5 %collective-permute-start.8 = (bf16[16,32,2,128]{3,1,2,0:T(8,128)(2,1)S(1)}, bf16[16,32,2,128]{3,1,2,0:T(8,128)(2,1)S(1)}, u32[]{:S(2)}, u32[]{:S(2)}) collective-permute-start(bf16[16,32,2,128]{3,1,2,0:T(8,128)(2,1)S(1)} %bitcast.338), channel_id=1, source_target_pairs={{0,1},{1,2},{2,3},{4,5},{5,6},{6,7},{8,9},{9,10},{10,11},{12,13},{... | collective-permute-start | bytes 786440 | tf_op jit(solution)/shard_map/ppermute | solution.py:23
  113.6 3.3 %copy-start.2 = (bf16[16,32,2,128]{3,2,1,0:T(2,128)(2,1)S(1)}, bf16[16,32,2,128]{3,2,1,0:T(2,128)(2,1)}, u32[]{:S(2)}) copy-start(bf16[16,32,2,128]{3,2,1,0:T(2,128)(2,1)} %param.7) | copy-start | bytes 786436
  113.6 3.3 %copy-start.10 = (f32[32]{0:T(128)S(1)}, f32[32]{0:T(128)}, u32[]{:S(2)}) copy-start(f32[32]{0:T(128)} %get-tuple-element.55) | copy-start | bytes 388
  113.6 3.3 %copy-start.12 = (f32[32]{0:T(128)S(1)}, f32[32]{0:T(128)}, u32[]{:S(2)}) copy-start(f32[32]{0:T(128)} %get-tuple-element.56) | copy-start | bytes 388
  113.6 3.3 %copy-start.14 = (f32[32]{0:T(128)S(1)}, f32[32]{0:T(128)}, u32[]{:S(2)}) copy-start(f32[32]{0:T(128)} %get-tuple-element.57) | copy-start | bytes 388
  113.6 3.3 %copy-start.16 = (f32[32]{0:T(128)S(1)}, f32[32]{0:T(128)}, u32[]{:S(2)}) copy-start(f32[32]{0:T(128)} %get-tuple-element.58) | copy-start | bytes 388
  113.6 3.3 %copy-start.18 = (f32[32]{0:T(128)S(1)}, f32[32]{0:T(128)}, u32[]{:S(2)}) copy-start(f32[32]{0:T(128)} %get-tuple-element.59) | copy-start | bytes 388
  113.6 3.3 %copy-start.20 = (f32[32]{0:T(128)S(1)}, f32[32]{0:T(128)}, u32[]{:S(2)}) copy-start(f32[32]{0:T(128)} %get-tuple-element.60) | copy-start | bytes 388
  113.6 3.3 %copy-start.22 = (f32[32]{0:T(128)S(1)}, f32[32]{0:T(128)}, u32[]{:S(2)}) copy-start(f32[32]{0:T(128)} %get-tuple-element.61) | copy-start | bytes 388
